TPU v7x, 256 devices: a whole 4x4x8 slice. The times are simulated.
256 devices in a mesh: pair: 32 (over z, x_lo, core), grp: 8 (over y, x_hi).
Axes of the slice: x: 4 (x_hi: 2, x_lo: 2; x = x_hi * 2 + x_lo), y: 4, z: 8, core: 2. Of those that a mesh axis runs over, the one named last changes fastest.
Arguments:
- amplitudes: float32 [8, 224, 2048], P('grp', 'pair'), may hold values from -6 to 6
- integrals: float32 [2048, 65536], P('grp', 'pair'), may hold values from -0.375 to 0.375
- owner_blocks: int32 [16], replicated, may hold values from 0 to 15, each once
- occ_pairs: int32 [8, 2, 224], P('grp'), may hold values from 0 to 63, as said below
- vir_pairs: int32 [2, 65536], replicated, may hold values from 0 to 511, as said below
- occ_energy: float32 [64], replicated, may hold values from -1.5 to -0.5
- vir_energy: float32 [512], replicated, may hold values from 0.2 to 1.5
Outputs:
- ladder: float32 [8, 224, 65536], P('grp', 'pair')
Inputs may be any that keep to these rules, and one draw needn't show every extreme that they name: `occ_pairs`: each column is a pair i<j; no pair occurs twice. `vir_pairs`: each column is a pair a<b; no pair occurs twice. `owner_blocks`: a permutation.
All inputs are finite; a program needn't handle non-finite values.
Results may differ from a plain program's by a relative error of at most 0.000071.
Values sent between devices are 32-bit elements; how exact they have to be, the bound alone decides.
No kernel may reach another device: no remote copies, remote signals or barrier semaphores. Data moves between devices by JAX's collectives and lax.ppermute only.
A program may use at most 64 MiB of HBM per device.

v0:
```python
import jax
import jax.numpy as jnp
from jax import lax
from jax.sharding import PartitionSpec as P


def pair_energies(energy, pairs):
    return jnp.take(energy, pairs[0]) + jnp.take(energy, pairs[1])


def on_device(amplitudes, integrals, owner_blocks, occ_pairs, vir_pairs, occ_energy, vir_energy):
    block = integrals.shape[0]
    columns = integrals.shape[1]
    groups = lax.axis_size("grp")
    nblocks = owner_blocks.shape[0]
    sub_width = block * groups // nblocks
    group_rows = lax.all_gather(amplitudes, "pair", axis=1, tiled=True)[0]
    piece = lax.all_gather(integrals, "grp", axis=0, tiled=True)
    count = piece.shape[0]
    rows = jnp.arange(count, dtype=jnp.int32)
    owner = jnp.take(owner_blocks, rows // sub_width)
    picked = owner * sub_width + rows % sub_width
    chosen = jnp.take(group_rows, picked, axis=1)
    work = jnp.dot(
        chosen, piece, precision=lax.Precision.HIGHEST, preferred_element_type=jnp.float32
    )
    occ_sum = pair_energies(occ_energy, occ_pairs[0])
    vir_local = lax.dynamic_slice_in_dim(vir_pairs, lax.axis_index("pair") * columns, columns, 1)
    vir_sum = pair_energies(vir_energy, vir_local)
    payload = work / (occ_sum[:, None] - vir_sum[None, :])
    return lax.all_to_all(payload[None], "pair", split_axis=1, concat_axis=2, tiled=True)


def solution(mesh):
    return jax.shard_map(
        on_device,
        mesh=mesh,
        in_specs=(
            P("grp", "pair", None),
            P("grp", "pair"),
            P(),
            P("grp", None, None),
            P(),
            P(),
            P(),
        ),
        out_specs=P("grp", "pair", None),
        check_vma=False,
    )
```

profile of v0, /device:TPU:1, one launch (start us, length us, event | category | flops | bytes accessed | tf_op | source)
XLA Modules:
  0.0 351.4 jit_solution(17929817763536348124)
XLA Ops:
  6.5 0.0 copy-start
  6.5 0.0 all-gather.3.cloned.1.call-start
  6.5 0.7 all-gather.3.cloned.1.call-update
  7.3 0.0 all-gather.5.cloned.1.call-start
  7.3 0.7 all-gather.5.cloned.1.call-update
  8.0 0.9 constant_dynamic-slice_fusion
  8.9 0.0 copy-done
  8.9 13.2 %gather_fusion.3 = f32[2048]{0:T(1024)S(1)} fusion(f32[512]{0:T(512)S(1)} %copy-done, s32[2048]{0:T(1024)S(1)} %fusion.16), kind=kCustom, calls=%fused_computation.1.clone | custom fusion | bytes 24576 | tf_op jit(solution)/shard_map/jit(_take)/gather | solution.py:8
  22.1 0.0 copy-start.3
  22.1 0.0 copy-start.1
  22.1 13.2 %gather_fusion.4 = f32[2048]{0:T(1024)S(1)} fusion(f32[512]{0:T(512)S(1)} %copy-done, s32[2048]{0:T(1024)S(1)} %fusion.17), kind=kCustom, calls=%fused_computation.3.clone | custom fusion | bytes 24576 | tf_op jit(solution)/shard_map/jit(_take)/gather | solution.py:8
  35.3 0.0 copy-done.3
  35.4 0.0 copy-start.2
  35.4 0.0 copy-done.1
  35.4 1.9 gather_fusion.1
  37.3 1.9 gather_fusion.2
  39.6 0.0 copy-done.2
  39.6 0.7 fusion.21
  40.3 4.4 %compare_select_fusion.2 = s32[2048,1]{0,1:T(1,128)S(1)} fusion(s32[]{:T(128)} %bitcast.9, s32[]{:T(128)} %bitcast.10, s32[]{:T(128)} %bitcast.11, s32[]{:T(128)} %bitcast.12, s32[]{:T(128)} %bitcast.13, s32[]{:T(128)} %bitcast.15, s32[]{:T(128)} %bitcast.14), kind=kLoop, calls=%fused_computation.21 | loop fusion | flops 47104 | bytes 8220 | tf_op jit(solution)/shard_map/jit(_take)/gather | solution.py:21
  44.8 5.7 %compare_and_fusion = (pred[2048]{0:T(1024)(128)(4,1)S(1)}, s32[2048]{0:T(1024)S(1)}) fusion(pred[2048]{0:T(1024)(128)(4,1)S(1)} %compare_reduce_fusion, pred[2048]{0:T(1024)(128)(4,1)S(1)} %compare_reduce_fusion.1, pred[2048]{0:T(1024)(128)(4,1)S(1)} %compare_reduce_fusion.2, pred[2048]{0:T(1024)(128)(4,1)S(1)} %compare_reduce_fusion.3, ...), kind=kLoop, calls=%fused_computation.55 | loop fusion | flops 73728 | bytes 36900 | tf_op jit(solution)/shard_map/jit(_take)/and | solution.py:23
  50.5 27.1 %all-gather.3.cloned.1.call-done = f32[1,224,2048]{2,0,1:T(1,128)} async-done(((f32[1,7,2048]{2,0,1:T(1,128)}), f32[1,224,2048]{2,0,1:T(1,128)}) %all-gather.3.cloned.1.call-update) | async-done | bytes 1835024 | tf_op jit(solution)/shard_map/all_gather | solution.py:17
  77.6 4.1 %copy.13 = f32[1,224,2048]{1,2,0:T(8,128)S(1)} copy(f32[1,224,2048]{2,0,1:T(1,128)} %all-gather.3.cloned.1.call-done) | data formatting | bytes 3670016 | tf_op jit(solution)/shard_map/all_gather | solution.py:17
  81.6 8.6 %gather_fusion = f32[2048,224]{1,0:T(8,128)} fusion(f32[224,2048]{0,1:T(8,128)S(1)} %bitcast.32, s32[2048]{0:T(1024)S(1)} %broadcast_clamp_fusion), kind=kCustom, calls=%fused_computation.4 | custom fusion | bytes 3678208 | tf_op jit(solution)/shard_map/jit(_take)/gather | solution.py:23
  90.2 175.9 %all-gather.5.cloned.1.call-done = f32[2048,2048]{1,0:T(8,128)} async-done(((f32[256,2048]{1,0:T(8,128)}), f32[2048,2048]{1,0:T(8,128)}) %all-gather.5.cloned.1.call-update) | async-done | bytes 16777232 | tf_op jit(solution)/shard_map/all_gather | solution.py:18
  266.1 20.5 %fusion = f32[1,224,2048]{2,1,0:T(8,128)S(1)} fusion(f32[2048,2048]{1,0:T(8,128)} %all-gather.5.cloned.1.call-done, f32[2048,224]{1,0:T(8,128)} %gather_fusion, pred[2048]{0:T(1024)(128)(4,1)S(1)} %get-tuple-element.6, f32[2048]{0:T(1024)S(1)} %select_add_fusion, f32[224]{0:T(256)S(1)} %fusion.18), kind=kOutput, calls=%fused_computation.6 | convolution fusion | flops 11275665408 | bytes 20458368 | tf_op jit(solution)/shard_map/dot_general | solution.py:24
  286.6 1.9 copy.14
  288.5 53.5 %all_to_all.18 = f32[1,224,2048]{2,0,1:T(1,128)S(1)} all-to-all(f32[1,224,2048]{2,0,1:T(1,128)S(1)} %copy.14), channel_id=1, replica_groups=mesh['pair'=32,'grp'=8] {'pair'}, dimensions={1} | all-to-all | bytes 3670016 | tf_op jit(solution)/shard_map/all_to_all | solution.py:31
  342.0 2.6 copy.16
  (20 shorter events, 0.5 us)
Async XLA Ops:
  6.5 2.4 copy-start
  6.5 71.0 %all-gather.3.cloned.1.call-start = ((), (), s32[]{:S(2)}) async-start(), calls=%async_computation.1 | async-start | bytes 1892352 | tf_op jit(solution)/shard_map/all_gather | solution.py:17
  7.3 258.8 %all-gather.5.cloned.1.call-start = ((), (), s32[]{:S(2)}) async-start(), calls=%async_computation.2 | async-start | bytes 18874368 | tf_op jit(solution)/shard_map/all_gather | solution.py:18
  22.1 13.2 %copy-start.3 = (s32[1,2,224]{2,1,0:T(2,128)S(1)}, s32[1,2,224]{2,1,0:T(2,128)}, u32[]{:S(2)}) copy-start(s32[1,2,224]{2,1,0:T(2,128)} %param.14) | copy-start | bytes 5380
  22.1 13.3 %copy-start.1 = (f32[64]{0:T(128)S(1)}, f32[64]{0:T(128)}, u32[]{:S(2)}) copy-start(f32[64]{0:T(128)} %param.16) | copy-start | bytes 772
  35.4 4.2 %copy-start.2 = (s32[16]{0:T(128)S(1)}, s32[16]{0:T(128)}, u32[]{:S(2)}) copy-start(s32[16]{0:T(128)} %param.13) | copy-start | bytes 196
Sparse Core Ops, SparseCore 0:
  9.2 68.3 all-gather.2
  80.2 185.8 all-gather.4
where the time goes:
time: 352 us; the launch traced here: 351 us
  waiting for transfers between devices  204 us (58%)
  blocking collectives  53.5 us (15%)
  local copies, waits for them, and re-layouts  48.8 us (14%)
  matrix products  20.5 us (6%)
  between operations  13.6 us (4%)
  other arithmetic  10.5 us (3%)
    all_gather x1, waiting for transfers between devices, on_device(): piece = lax.all_gather(integrals, 'grp', axis=0, tiled=True)  176 us
    all_to_all x1, blocking collectives, on_device(): lax.all_to_all(payload[None], 'pair', split_axis=1, concat_axis=2, tiled=...  53.5 us
    gather x4, local copies, waits for them, and re-layouts, pair_energies(): return jnp.take(energy, pairs[0]) + jnp.take(energy, pairs[1])  30.1 us
    all_gather x1, waiting for transfers between devices, on_device(): group_rows = lax.all_gather(amplitudes, 'pair', axis=1, tiled=True)[0]  27.1 us
    dot_general x1, matrix products, on_device(): jnp.dot(chosen, piece, precision=lax.Precision.HIGHEST, preferred_element...  20.5 us
    gather x1, local copies, waits for them, and re-layouts, on_device(): chosen = jnp.take(group_rows, picked, axis=1)  8.56 us
  transfers between devices with their start and end apart: 2, of which 2 were waited for; matrix products, arithmetic and copies ran while one was open for 16% of the time, Pallas kernels for 0%

commit v1 on v0

--- a/solution.py
+++ b/solution.py
@@ -15,7 +15,9 @@
     nblocks = owner_blocks.shape[0]
     sub_width = block * groups // nblocks
     group_rows = lax.all_gather(amplitudes, "pair", axis=1, tiled=True)[0]
-    piece = lax.all_gather(integrals, "grp", axis=0, tiled=True)
+    piece = jnp.concatenate(
+        lax.all_to_all(jnp.stack([integrals] * lax.axis_size("grp")), "grp", 0, 0), axis=0
+    )
     count = piece.shape[0]
     rows = jnp.arange(count, dtype=jnp.int32)
     owner = jnp.take(owner_blocks, rows // sub_width)

time: 352 us -> 304 us (0.86)
  waiting for transfers between devices: 204 us -> 138 us
  local copies, waits for them, and re-layouts: 48.8 us -> 58.3 us
  starting transfers between devices: 0.04 us -> 7.51 us
    all_gather x1 -> x0, waiting for transfers between devices: 176 us -> none  [on_device(): piece = lax.all_gather(integrals, 'grp', axis=0, tiled=True)]
    all_to_all x0 -> x1, waiting for transfers between devices: none -> 110 us  [on_device(): lax.all_to_all(jnp.stack([integrals] * lax.axis_size('grp')), 'grp', 0, 0)]
    another operation x0 -> x1, local copies, waits for them, and re-layouts: none -> 9.45 us  [on_device(): jnp.stack([integrals] * lax.axis_size('grp'))]
    all_to_all x0 -> x1, starting transfers between devices: none -> 7.47 us  [on_device(): lax.all_to_all(jnp.stack([integrals] * lax.axis_size('grp')), 'grp', 0, 0)]
  transfers between devices with their start and end apart: 2 -> 2, of which waited for: 2 -> 2; matrix products, arithmetic and copies ran while one was open for 16% -> 18% of each run, Pallas kernels for 0% -> 0%
where the time goes in v1:
time: 304 us
  waiting for transfers between devices  138 us (45%)
  local copies, waits for them, and re-layouts  58.3 us (19%)
  blocking collectives  54.5 us (18%)
  matrix products  20.5 us (7%)
  between operations  13.6 us (4%)
  other arithmetic  10.8 us (4%)
  starting transfers between devices  7.51 us (2%)
    all_to_all x1, waiting for transfers between devices, on_device(): lax.all_to_all(jnp.stack([integrals] * lax.axis_size('grp')), 'grp', 0, 0)  110 us
    all_to_all x1, blocking collectives, on_device(): lax.all_to_all(payload[None], 'pair', split_axis=1, concat_axis=2, tiled=...  54.5 us
    gather x4, local copies, waits for them, and re-layouts, pair_energies(): return jnp.take(energy, pairs[0]) + jnp.take(energy, pairs[1])  30.1 us
    all_gather x1, waiting for transfers between devices, on_device(): group_rows = lax.all_gather(amplitudes, 'pair', axis=1, tiled=True)[0]  27.4 us
    dot_general x1, matrix products, on_device(): jnp.dot(chosen, piece, precision=lax.Precision.HIGHEST, preferred_element...  20.5 us
    another operation x1, local copies, waits for them, and re-layouts, on_device(): jnp.stack([integrals] * lax.axis_size('grp'))  9.45 us
    gather x1, local copies, waits for them, and re-layouts, on_device(): chosen = jnp.take(group_rows, picked, axis=1)  8.55 us
    all_to_all x1, starting transfers between devices, on_device(): lax.all_to_all(jnp.stack([integrals] * lax.axis_size('grp')), 'grp', 0, 0)  7.47 us
  transfers between devices with their start and end apart: 2, of which 2 were waited for; matrix products, arithmetic and copies ran while one was open for 18% of the time, Pallas kernels for 0%

profile of v1, /device:TPU:1, one launch (start us, length us, event | category | flops | bytes accessed | tf_op | source)
XLA Modules:
  0.0 303.5 jit_solution(1069842612828746574)
XLA Ops:
  6.5 0.0 copy-start
  6.5 9.4 %stack.2 = f32[8,256,2048]{2,1,0:T(8,128)} broadcast(f32[256,2048]{1,0:T(8,128)} %param.12), dimensions={1,2} | broadcast | bytes 18874368 | tf_op jit(solution)/shard_map/stack | solution.py:19
  16.0 7.5 %all-to-all-start = ((f32[8,256,2048]{2,1,0:T(8,128)}), f32[8,256,2048]{2,1,0:T(8,128)}, u32[]{:S(2)}, u32[]{:S(2)}) async-start(f32[8,256,2048]{2,1,0:T(8,128)} %stack.2), calls=%async_computation | async-start | bytes 33554432 | tf_op jit(solution)/shard_map/all_to_all | solution.py:19
  23.5 0.0 all-gather.2.cloned.1.call-start
  23.5 0.7 all-gather.2.cloned.1.call-update
  24.2 0.9 constant_dynamic-slice_fusion
  25.1 0.0 copy-done
  25.1 13.2 %gather_fusion.4 = f32[2048]{0:T(1024)S(1)} fusion(f32[512]{0:T(512)S(1)} %copy-done, s32[2048]{0:T(1024)S(1)} %fusion.17), kind=kCustom, calls=%fused_computation.3.clone | custom fusion | bytes 24576 | tf_op jit(solution)/shard_map/jit(_take)/gather | solution.py:8
  38.3 0.0 copy-start.3
  38.3 0.0 copy-start.1
  38.3 13.2 %gather_fusion.3 = f32[2048]{0:T(1024)S(1)} fusion(f32[512]{0:T(512)S(1)} %copy-done, s32[2048]{0:T(1024)S(1)} %fusion.16), kind=kCustom, calls=%fused_computation.1.clone | custom fusion | bytes 24576 | tf_op jit(solution)/shard_map/jit(_take)/gather | solution.py:8
  51.5 0.0 copy-done.3
  51.5 0.0 copy-start.2
  51.6 0.0 copy-done.1
  51.6 1.9 gather_fusion.1
  53.5 1.9 gather_fusion.2
  55.8 0.0 copy-done.2
  55.8 0.7 fusion.21
  56.5 4.5 %compare_select_fusion.2 = s32[2048,1]{0,1:T(1,128)S(1)} fusion(s32[]{:T(128)} %bitcast.9, s32[]{:T(128)} %bitcast.10, s32[]{:T(128)} %bitcast.11, s32[]{:T(128)} %bitcast.12, s32[]{:T(128)} %bitcast.13, s32[]{:T(128)} %bitcast.15, s32[]{:T(128)} %bitcast.14), kind=kLoop, calls=%fused_computation.21 | loop fusion | flops 47104 | bytes 8220 | tf_op jit(solution)/shard_map/jit(_take)/gather | solution.py:23
  61.0 5.9 %compare_and_fusion = (pred[2048]{0:T(1024)(128)(4,1)S(1)}, s32[2048]{0:T(1024)S(1)}) fusion(pred[2048]{0:T(1024)(128)(4,1)S(1)} %compare_reduce_fusion, pred[2048]{0:T(1024)(128)(4,1)S(1)} %compare_reduce_fusion.1, pred[2048]{0:T(1024)(128)(4,1)S(1)} %compare_reduce_fusion.2, pred[2048]{0:T(1024)(128)(4,1)S(1)} %compare_reduce_fusion.3, ...), kind=kLoop, calls=%fused_computation.55 | loop fusion | flops 73728 | bytes 36900 | tf_op jit(solution)/shard_map/jit(_take)/and | solution.py:25
  66.9 27.4 %all-gather.2.cloned.1.call-done = f32[1,224,2048]{2,0,1:T(1,128)} async-done(((f32[1,7,2048]{2,0,1:T(1,128)}), f32[1,224,2048]{2,0,1:T(1,128)}) %all-gather.2.cloned.1.call-update) | async-done | bytes 1835024 | tf_op jit(solution)/shard_map/all_gather | solution.py:17
  94.3 4.1 %copy.13 = f32[1,224,2048]{1,2,0:T(8,128)S(1)} copy(f32[1,224,2048]{2,0,1:T(1,128)} %all-gather.2.cloned.1.call-done) | data formatting | bytes 3670016 | tf_op jit(solution)/shard_map/all_gather | solution.py:17
  98.3 8.5 %gather_fusion = f32[2048,224]{1,0:T(8,128)} fusion(f32[224,2048]{0,1:T(8,128)S(1)} %bitcast.33, s32[2048]{0:T(1024)S(1)} %broadcast_clamp_fusion), kind=kCustom, calls=%fused_computation.4 | custom fusion | bytes 3678208 | tf_op jit(solution)/shard_map/jit(_take)/gather | solution.py:25
  106.9 110.3 %all-to-all-done = f32[8,256,2048]{2,1,0:T(8,128)} async-done(((f32[8,256,2048]{2,1,0:T(8,128)}), f32[8,256,2048]{2,1,0:T(8,128)}, u32[]{:S(2)}, u32[]{:S(2)}) %all-to-all-start) | async-done | bytes 16777248 | tf_op jit(solution)/shard_map/all_to_all | solution.py:19
  217.2 20.5 %fusion = f32[1,224,2048]{2,1,0:T(8,128)S(1)} fusion(f32[2048,2048]{1,0:T(8,128)} %bitcast.20, f32[2048,224]{1,0:T(8,128)} %gather_fusion, pred[2048]{0:T(1024)(128)(4,1)S(1)} %get-tuple-element.6, f32[2048]{0:T(1024)S(1)} %select_add_fusion, f32[224]{0:T(256)S(1)} %fusion.18), kind=kOutput, calls=%fused_computation.6 | convolution fusion | flops 11275665408 | bytes 20458368 | tf_op jit(solution)/shard_map/dot_general | solution.py:26
  237.7 1.9 copy.14
  239.6 54.5 %all_to_all.23 = f32[1,224,2048]{2,0,1:T(1,128)S(1)} all-to-all(f32[1,224,2048]{2,0,1:T(1,128)S(1)} %copy.14), channel_id=1, replica_groups=mesh['pair'=32,'grp'=8] {'pair'}, dimensions={1} | all-to-all | bytes 3670016 | tf_op jit(solution)/shard_map/all_to_all | solution.py:33
  294.1 2.6 copy.16
  (20 shorter events, 0.5 us)
Async XLA Ops:
  6.5 18.6 %copy-start = (f32[512]{0:T(512)S(1)}, f32[512]{0:T(512)}, u32[]{:S(2)}) copy-start(f32[512]{0:T(512)} %param.17) | copy-start | bytes 6148
  16.0 201.2 %all-to-all-start = ((f32[8,256,2048]{2,1,0:T(8,128)}), f32[8,256,2048]{2,1,0:T(8,128)}, u32[]{:S(2)}, u32[]{:S(2)}) async-start(f32[8,256,2048]{2,1,0:T(8,128)} %stack.2), calls=%async_computation | async-start | bytes 33554432 | tf_op jit(solution)/shard_map/all_to_all | solution.py:19
  23.5 70.8 %all-gather.2.cloned.1.call-start = ((), (), s32[]{:S(2)}) async-start(), calls=%async_computation.2 | async-start | bytes 1892352 | tf_op jit(solution)/shard_map/all_gather | solution.py:17
  38.3 13.2 %copy-start.3 = (s32[1,2,224]{2,1,0:T(2,128)S(1)}, s32[1,2,224]{2,1,0:T(2,128)}, u32[]{:S(2)}) copy-start(s32[1,2,224]{2,1,0:T(2,128)} %param.14) | copy-start | bytes 5380
  38.3 13.3 %copy-start.1 = (f32[64]{0:T(128)S(1)}, f32[64]{0:T(128)}, u32[]{:S(2)}) copy-start(f32[64]{0:T(128)} %param.16) | copy-start | bytes 772
  51.5 4.2 %copy-start.2 = (s32[16]{0:T(128)S(1)}, s32[16]{0:T(128)}, u32[]{:S(2)}) copy-start(s32[16]{0:T(128)} %param.13) | copy-start | bytes 196
Sparse Core Ops, SparseCore 0:
  26.1 68.1 all-gather.1
